TPU v7x, 512 devices: a whole 4x8x8 slice. The times are simulated.
512 devices in a mesh: group: 16 (over x_lo, z), row: 32 (over x_hi, y, core).
Axes of the slice: x: 4 (x_hi: 2, x_lo: 2; x = x_hi * 2 + x_lo), y: 8, z: 8, core: 2. Of those that a mesh axis runs over, the one named last changes fastest.
Arguments:
- features: float32 [98304, 2048], P('row', 'group'), may hold values from -6 to 6
- feature_id: int32 [2048], P('group'), may hold values from 0 to 2047, each once
- feature_shift: float32 [2048], replicated, may hold values from -3 to 3
- feature_scale: float32 [2048], replicated, may hold values from 0.25 to 2
- proj_weight: bfloat16 [2048, 256], P('group'), may hold values from -0.5 to 0.5
- row_slot: int32 [32, 3072], P('row'), may hold values from 0 to 3071, each once within a row
- down_weight: bfloat16 [2, 4096, 128], P(None, 'row'), may hold values from -0.09375 to 0.09375
- up_weight: bfloat16 [2, 4096, 128], P(None, 'row'), may hold values from -0.5 to 0.5
- cross_bias: float32 [2, 4096], replicated, may hold values from -3 to 3
- head_weight: float32 [4096], replicated, may hold values from -0.09375 to 0.09375
- labels: int32 [98304], P(('group', 'row')), may hold values 0 or 1
Outputs:
- logits: float32 [98304], P(('group', 'row'))
- grad_down: float32 [2, 4096, 128], P(None, 'row')
- grad_up: float32 [2, 4096, 128], P(None, 'row')
- grad_bias: float32 [2, 4096], replicated
- grad_proj: float32 [2048, 256], P('group')
Inputs may be any that keep to these rules, and one draw needn't show every extreme that they name: Each row of row_slot holds every number 0 .. 3071 once. feature_id holds every number 0 .. 2047 once.
All inputs are finite; a program needn't handle non-finite values. No bound on the sum of `labels` on one device may be relied on, other than what follows from the above.
Results may differ from a plain program's by a relative error of at most 0.02.
Values may be sent and summed in bfloat16 or wider, within the bound.
No kernel may reach another device: no remote copies, remote signals or barrier semaphores. Data moves between devices by JAX's collectives and lax.ppermute only.
A program may use at most 64 MiB of HBM per device.

v0:
```python
import jax
import jax.numpy as jnp
from jax import lax
from jax.sharding import PartitionSpec as P


def column_table(feature_id, lookup_table):
    columns = jnp.arange(lookup_table.shape[0], dtype=jnp.int32)
    picker = (feature_id[:, None] == columns[None, :]).astype(jnp.float32)
    return jnp.dot(picker, lookup_table, precision=lax.Precision.HIGHEST)


def exchange_sum(partial, axis, count):
    pieces = partial.reshape(count, -1)
    mine = jnp.sum(lax.all_to_all(pieces, axis, 0, 0, tiled=True), axis=0)
    spread = jnp.broadcast_to(mine[None], pieces.shape)
    return lax.all_to_all(spread, axis, 0, 0, tiled=True).reshape(partial.shape)


def group_all_reduce(rows, groups):
    stacked, height, width = rows.shape
    pieces = rows.reshape(stacked, groups, height // groups, width).transpose(1, 0, 2, 3)
    mine = jnp.sum(lax.all_to_all(pieces, "group", 0, 0, tiled=True).astype(jnp.float32), axis=0)
    spread = jnp.broadcast_to(mine.astype(jnp.bfloat16)[None], pieces.shape)
    gathered = lax.all_to_all(spread, "group", 0, 0, tiled=True).astype(jnp.float32)
    return gathered.transpose(1, 0, 2, 3).reshape(rows.shape)


def body(
    features,
    feature_id,
    feature_shift,
    feature_scale,
    proj_weight,
    row_slot,
    down_weight,
    up_weight,
    cross_bias,
    head_weight,
    labels,
):
    layers = down_weight.shape[0]
    groups = lax.axis_size("group")
    row_count = labels.shape[0]
    feature_stats = column_table(feature_id, jnp.stack([feature_shift, feature_scale], axis=1))
    normed = ((features - feature_stats[:, 0][None, :]) * feature_stats[:, 1][None, :]).astype(
        jnp.bfloat16
    )
    ordered = jnp.zeros_like(normed).at[row_slot[0]].set(normed)
    projected = jnp.dot(ordered, proj_weight, preferred_element_type=jnp.float32).astype(
        jnp.bfloat16
    )
    first = lax.all_to_all(projected, "group", split_axis=0, concat_axis=1, tiled=True)
    first_wide = first.astype(jnp.float32)
    crossed = first
    stored = []
    weights_full = lax.all_gather(
        jnp.concatenate([down_weight, up_weight], axis=0), "row", axis=1, tiled=True
    )
    for layer_index in range(layers):
        down_full, up_full = (weights_full[layer_index], weights_full[layers + layer_index])
        hidden = jnp.dot(crossed, down_full, preferred_element_type=jnp.float32).astype(
            jnp.bfloat16
        )
        mixture = lax.dot_general(
            hidden, up_full, (((1,), (1,)), ((), ())), preferred_element_type=jnp.float32
        )
        mixture = mixture + cross_bias[layer_index][None, :]
        stored.append((crossed, hidden, mixture, down_full, up_full))
        crossed = (first_wide * mixture + crossed.astype(jnp.float32)).astype(jnp.bfloat16)
    logits = jnp.sum(crossed.astype(jnp.float32) * head_weight[None, :], axis=1)
    total_rows = row_count * groups * lax.axis_size("row")
    loss_scale = 2.0 * (crossed.shape[1] / total_rows) ** 0.5
    logit_grad = (jax.nn.sigmoid(logits) - labels.astype(jnp.float32)) * loss_scale
    back = (logit_grad[:, None] * head_weight[None, :]).astype(jnp.bfloat16)
    first_grad = jnp.zeros(first.shape, jnp.float32)
    up_parts = [None] * layers
    down_parts = [None] * layers
    bias_terms = [None] * layers
    for layer_index in reversed(range(layers)):
        crossed_in, hidden, mixture, down_full, up_full = stored[layer_index]
        back_wide = back.astype(jnp.float32)
        first_grad = first_grad + back_wide * mixture
        mix_grad = (back_wide * first_wide).astype(jnp.bfloat16)
        up_term = lax.dot_general(
            mix_grad, hidden, (((0,), (0,)), ((), ())), preferred_element_type=jnp.float32
        )
        bias_terms[layer_index] = mix_grad
        hidden_grad = jnp.dot(mix_grad, up_full, preferred_element_type=jnp.float32).astype(
            jnp.bfloat16
        )
        down_term = lax.dot_general(
            crossed_in, hidden_grad, (((0,), (0,)), ((), ())), preferred_element_type=jnp.float32
        )
        through = lax.dot_general(
            hidden_grad, down_full, (((1,), (1,)), ((), ())), preferred_element_type=jnp.float32
        )
        back = (back_wide + through).astype(jnp.bfloat16)
        up_parts[layer_index] = up_term
        down_parts[layer_index] = down_term
    slab = jnp.stack(up_parts + down_parts).astype(jnp.bfloat16)
    slab, bias_terms = lax.optimization_barrier((slab, bias_terms))
    bias_terms = [jnp.sum(mix_grad.astype(jnp.float32), axis=0) for mix_grad in bias_terms]
    weight_rows = lax.psum_scatter(slab, "row", scatter_dimension=1, tiled=True)
    first_grad = (first_grad + back.astype(jnp.float32)).astype(jnp.bfloat16)
    owner_grad = lax.all_to_all(first_grad, "group", split_axis=1, concat_axis=0, tiled=True)
    proj_term = lax.dot_general(
        ordered, owner_grad, (((0,), (0,)), ((), ())), preferred_element_type=jnp.float32
    )
    row_count_axis = lax.axis_size("row")
    bias_all = jnp.stack(bias_terms)
    proj_pieces = proj_term.reshape(row_count_axis, -1)
    bias_pieces = bias_all.reshape(layers, row_count_axis, -1).transpose(1, 0, 2)
    bias_pieces = bias_pieces.reshape(row_count_axis, -1)
    split = proj_pieces.shape[1]
    row_mine = jnp.sum(
        lax.all_to_all(
            jnp.concatenate([proj_pieces, bias_pieces], axis=1), "row", 0, 0, tiled=True
        ),
        axis=0,
    )
    bias_chunk = exchange_sum(row_mine[split:], "group", groups)
    last = jnp.concatenate([row_mine[:split], bias_chunk])
    last_all = lax.all_to_all(
        jnp.broadcast_to(last[None], (row_count_axis,) + last.shape), "row", 0, 0, tiled=True
    )
    grad_proj = last_all[:, :split].reshape(proj_term.shape)
    grad_bias = (
        last_all[:, split:]
        .reshape(row_count_axis, layers, -1)
        .transpose(1, 0, 2)
        .reshape(bias_all.shape)
    )
    weight_rows, grad_proj, grad_bias = lax.optimization_barrier(
        (weight_rows, grad_proj, grad_bias)
    )
    weight_sums = group_all_reduce(weight_rows, groups)
    grad_up, grad_down = (weight_sums[:layers], weight_sums[layers:])
    return (logits, grad_down, grad_up, grad_bias, grad_proj)


def solution(mesh):
    in_specs = (
        P("row", "group"),
        P("group"),
        P(),
        P(),
        P("group", None),
        P("row", None),
        P(None, "row", None),
        P(None, "row", None),
        P(),
        P(),
        P(("group", "row")),
    )
    out_specs = (
        P(("group", "row")),
        P(None, "row", None),
        P(None, "row", None),
        P(),
        P("group", None),
    )
    return jax.shard_map(body, mesh=mesh, in_specs=in_specs, out_specs=out_specs, check_vma=False)
```

profile of v0, /device:TPU:16, one launch (start us, length us, event | category | flops | bytes accessed | tf_op | source)
XLA Modules:
  0.0 299.1 jit_solution(5511135230182900880)
XLA Ops:
  7.2 0.0 copy-start
  7.2 0.0 all-gather.2.cloned.1.call-start
  7.2 1.5 pad_maximum_fusion.2
  8.8 0.0 all-gather.2.cloned.1.call-update
  8.8 1.4 fusion.17
  10.2 0.7 compare_select_fusion
  10.9 8.9 %scatter_custom_fusion = bf16[3072,128]{1,0:T(8,128)(2,1)S(1)} fusion(s32[3072]{0:T(1024)S(1)} %bitcast.121, f32[3072,128]{1,0:T(8,128)} %param.11, f32[128]{0:T(128)S(1)} %get-tuple-element.24, f32[128]{0:T(128)S(1)} %get-tuple-element.23, bf16[]{:T(256)} %constant.1.clone.1), kind=kCustom, calls=%fused_computation.52 | custom fusion | flops 1179648 | bytes 2360322 | tf_op jit(solution)/shard_map/scatter | solution.py:49
  19.8 0.0 copy-done
  19.8 0.0 copy-start.3
  19.8 0.0 copy-start.5
  19.8 0.0 copy-start.6
  19.9 1.7 convolution_convert_fusion.4
  21.6 0.0 copy-done.3
  21.6 11.4 %all-to-all-start = ((bf16[16,192,256]{2,1,0:T(8,128)(2,1)}), bf16[16,192,256]{2,1,0:T(8,128)(2,1)S(1)}, u32[]{:S(2)}, u32[]{:S(2)}) async-start(bf16[16,192,256]{2,1,0:T(8,128)(2,1)} %bitcast.6), calls=%async_computation | async-start | bytes 3145728 | tf_op jit(solution)/shard_map/all_to_all | solution.py:53
  33.0 0.2 reduce-scatter.2.cloned.1.call-start
  33.2 0.0 copy-done.5
  33.2 0.0 copy-done.6
  33.3 37.7 %all-to-all-done = bf16[16,192,256]{2,1,0:T(8,128)(2,1)S(1)} async-done(((bf16[16,192,256]{2,1,0:T(8,128)(2,1)}), bf16[16,192,256]{2,1,0:T(8,128)(2,1)S(1)}, u32[]{:S(2)}, u32[]{:S(2)}) %all-to-all-start) | async-done | bytes 1572896 | tf_op jit(solution)/shard_map/all_to_all | solution.py:53
  71.0 0.2 copy.47
  71.2 37.0 %all-gather.2.cloned.1.call-done = bf16[4,4096,128]{2,1,0:T(8,128)(2,1)} async-done(((bf16[4,128,128]{2,1,0:T(8,128)(2,1)}), bf16[4,4096,128]{2,1,0:T(8,128)(2,1)}) %all-gather.2.cloned.1.call-update) | async-done | bytes 4194320 | tf_op jit(solution)/shard_map/all_gather | solution.py:57
  108.1 1.8 convolution_convert_fusion.8
  109.9 0.0 copy-start.4
  109.9 3.8 %fusion.11 = (bf16[192,4096]{1,0:T(8,128)(2,1)S(1)}, f32[192,4096]{1,0:T(8,128)}) fusion(bf16[192,4096]{1,0:T(8,128)(2,1)S(1)} %bitcast.103, f32[4096]{0:T(1024)S(1)} %bitcast.116, bf16[192,128]{1,0:T(8,128)(2,1)S(1)} %convolution_convert_fusion.8, bf16[4,4096,128]{2,1,0:T(8,128)(2,1)} %all-gather.2.cloned.1.call-done), kind=kOutput, calls=%fused_computation.28 | convolution fusion | flops 205258752 | bytes 7405568 | tf_op jit(solution)/shard_map/dot_general | solution.py:65
  113.7 0.6 convolution_convert_fusion.7
  114.3 0.0 copy-start.8
  114.3 2.7 multiply_reduce_fusion
  117.0 0.6 fusion.16
  117.7 0.2 copy.48
  117.8 0.6 convolution_convert_fusion.6
  118.4 0.8 fusion.9
  119.2 2.5 fusion.15
  121.7 0.8 fusion.6
  122.4 0.6 convolution_convert_fusion.5
  123.0 0.8 fusion.8
  123.8 0.8 fusion.7
  124.6 2.2 pad_maximum_fusion
  126.8 0.0 reduce-scatter.2.cloned.1.call-update
  126.8 4.9 %fusion.5 = bf16[192,4096]{1,0:T(8,128)(2,1)S(1)} fusion(f32[192,4096]{1,0:T(8,128)} %get-tuple-element.29, bf16[192,128]{1,0:T(8,128)(2,1)S(1)} %convolution_convert_fusion.5, f32[192,4096]{1,0:T(8,128)} %get-tuple-element.28, f32[192,4096]{1,0:T(8,128)} %get-tuple-element.26, f32[192]{0:T(256)S(1)} %fusion.26, f32[4096]{0:T(1024)S(1)} %copy-done.5, ...), kind=kOutput, calls=%fused_computation.15 | convolution fusion | flops 209977344 | bytes 12124928 | tf_op jit(solution)/shard_map/dot_general | solution.py:95
  131.8 1.3 copy.55
  133.1 7.5 %all-to-all-start.1 = ((bf16[192,16,256]{2,0,1:T(8,128)(2,1)}), bf16[192,16,256]{2,0,1:T(8,128)(2,1)}, u32[]{:S(2)}, u32[]{:S(2)}) async-start(bf16[192,16,256]{2,0,1:T(8,128)(2,1)} %bitcast.108), calls=%async_computation.2 | async-start | bytes 3145728 | tf_op jit(solution)/shard_map/all_to_all | solution.py:106
  140.6 0.0 copy-done.2
  140.6 0.5 convert_reduce_fusion
  141.2 38.0 %all-to-all-done.1 = bf16[192,16,256]{2,0,1:T(8,128)(2,1)} async-done(((bf16[192,16,256]{2,0,1:T(8,128)(2,1)}), bf16[192,16,256]{2,0,1:T(8,128)(2,1)}, u32[]{:S(2)}, u32[]{:S(2)}) %all-to-all-start.1) | async-done | bytes 1572896 | tf_op jit(solution)/shard_map/all_to_all | solution.py:106
  179.1 2.1 fusion.29
  181.3 0.1 all_to_all.64
  181.4 18.1 %all_to_all.81 = f32[32,1,1280]{2,1,0:T(1,128)S(1)} all-to-all(f32[32,1,1280]{2,1,0:T(1,128)S(1)} %all_to_all.64), channel_id=1, replica_groups=mesh['group'=16,'row'=32] {'row'}, dimensions={0} | all-to-all | bytes 327680 | tf_op jit(solution)/shard_map/all_to_all | solution.py:117
  199.5 0.1 reduce_sum.60
  199.6 0.1 all_to_all.66
  199.7 13.0 %all_to_all.82 = f32[16,1,16]{2,1,0:T(1,128)S(1)} all-to-all(f32[16,1,16]{2,1,0:T(1,128)S(1)} %all_to_all.66), channel_id=1, replica_groups=mesh['group'=16,'row'=32] {'group'}, dimensions={0} | all-to-all | bytes 2048 | tf_op jit(solution)/shard_map/all_to_all | solution.py:15
  212.7 0.6 broadcast_in_dim.9
  213.3 3.5 %all-to-all-start.4 = ((f32[16,1,16]{2,1,0:T(1,128)}), f32[16,1,16]{2,1,0:T(1,128)S(1)}, u32[]{:S(2)}, u32[]{:S(2)}) async-start(f32[16,1,16]{2,1,0:T(1,128)} %broadcast_in_dim.9), calls=%async_computation.5 | async-start | bytes 16384 | tf_op jit(solution)/shard_map/all_to_all | solution.py:17
  216.8 8.3 %all-to-all-done.4 = f32[16,1,16]{2,1,0:T(1,128)S(1)} async-done(((f32[16,1,16]{2,1,0:T(1,128)}), f32[16,1,16]{2,1,0:T(1,128)S(1)}, u32[]{:S(2)}, u32[]{:S(2)}) %all-to-all-start.4) | async-done | bytes 1056 | tf_op jit(solution)/shard_map/all_to_all | solution.py:17
  225.1 0.5 broadcast.39
  225.6 0.7 reduce.6
  226.3 0.1 reshape.117
  226.4 0.1 broadcast_in_dim.10
  226.5 15.9 %all_to_all.83 = f32[32,1,1280]{2,1,0:T(1,128)S(1)} all-to-all(f32[32,1,1280]{2,1,0:T(1,128)S(1)} %broadcast_in_dim.10), channel_id=1, replica_groups=mesh['group'=16,'row'=32] {'row'}, dimensions={0} | all-to-all | bytes 327680 | tf_op jit(solution)/shard_map/all_to_all | solution.py:124
  242.4 0.7 reshape.118
  243.1 0.6 reshape.119
  243.8 19.4 %reduce-scatter.2.cloned.1.call-done = bf16[4,128,128]{2,1,0:T(8,128)(2,1)} async-done(((bf16[4,4096,128]{2,1,0:T(8,128)(2,1)}), bf16[4,128,128]{2,1,0:T(8,128)(2,1)}) %reduce-scatter.2.cloned.1.call-update) | async-done | bytes 131088 | tf_op jit(solution)/shard_map/reduce_scatter | solution.py:104
  263.2 0.9 copy_bitcast_fusion.2
  264.1 15.7 %all_to_all.84 = bf16[16,4,8,128]{3,2,1,0:T(8,128)(2,1)S(1)} all-to-all(bf16[16,4,8,128]{3,2,1,0:T(8,128)(2,1)S(1)} %copy_bitcast_fusion.2), channel_id=1, replica_groups=mesh['group'=16,'row'=32] {'group'}, dimensions={0} | all-to-all | bytes 262144 | tf_op jit(solution)/shard_map/all_to_all | solution.py:23
  279.9 11.6 %all_to_all.85 = bf16[16,4,8,128]{3,2,1,0:T(8,128)(2,1)S(1)} all-to-all(bf16[16,4,8,128]{3,2,1,0:T(8,128)(2,1)S(1)} %broadcast_in_dim.11), channel_id=1, replica_groups=mesh['group'=16,'row'=32] {'group'}, dimensions={0} | all-to-all | bytes 262144 | tf_op jit(solution)/shard_map/all_to_all | solution.py:25
  291.5 0.7 slice_bitcast_fusion.12
  (25 shorter events, 0.3 us)
Async XLA Ops:
  7.2 12.7 %copy-start = (bf16[128,256]{1,0:T(8,128)(2,1)S(1)}, bf16[128,256]{1,0:T(8,128)(2,1)}, u32[]{:S(2)}) copy-start(bf16[128,256]{1,0:T(8,128)(2,1)} %param.15) | copy-start | bytes 196612
  7.2 101.0 %all-gather.2.cloned.1.call-start = ((), (), s32[]{:S(2)}) async-start(), calls=%async_computation.9 | async-start | bytes 4325376 | tf_op jit(solution)/shard_map/all_gather | solution.py:57
  19.8 1.8 copy-start.3
  19.8 13.3 %copy-start.5 = (f32[4096]{0:T(1024)S(1)}, f32[4096]{0:T(1024)}, u32[]{:S(2)}) copy-start(f32[4096]{0:T(1024)} %param.20) | copy-start | bytes 49156
  19.8 13.4 %copy-start.6 = (f32[2,4096]{1,0:T(2,128)S(1)}, f32[2,4096]{1,0:T(2,128)}, u32[]{:S(2)}) copy-start(f32[2,4096]{1,0:T(2,128)} %param.19) | copy-start | bytes 98308
  21.6 49.4 %all-to-all-start = ((bf16[16,192,256]{2,1,0:T(8,128)(2,1)}), bf16[16,192,256]{2,1,0:T(8,128)(2,1)S(1)}, u32[]{:S(2)}, u32[]{:S(2)}) async-start(bf16[16,192,256]{2,1,0:T(8,128)(2,1)} %bitcast.6), calls=%async_computation | async-start | bytes 3145728 | tf_op jit(solution)/shard_map/all_to_all | solution.py:53
  33.0 230.2 %reduce-scatter.2.cloned.1.call-start = ((), (), s32[]{:S(2)}) async-start(), calls=%async_computation.10 | async-start | bytes 4325376 | tf_op jit(solution)/shard_map/reduce_scatter | solution.py:104
  109.9 3.8 %copy-start.4 = (bf16[4,4096,128]{2,1,0:T(8,128)(2,1)S(1)}, bf16[4,4096,128]{2,1,0:T(8,128)(2,1)}, u32[]{:S(2)}) copy-start(bf16[4,4096,128]{2,1,0:T(8,128)(2,1)} %all-gather.2.cloned.1.call-done) | copy-start | bytes 12582916
  114.3 2.7 copy-start.8
  117.0 0.8 copy-start.7
  121.7 2.1 copy-start.1
  131.7 8.9 %copy-start.2 = (bf16[192,4096]{1,0:T(8,128)(2,1)S(1)}, bf16[192,4096]{1,0:T(8,128)(2,1)}, u32[]{:S(2)}) copy-start(bf16[192,4096]{1,0:T(8,128)(2,1)} %copy-done.1) | copy-start | bytes 4718596
  133.1 46.0 %all-to-all-start.1 = ((bf16[192,16,256]{2,0,1:T(8,128)(2,1)}), bf16[192,16,256]{2,0,1:T(8,128)(2,1)}, u32[]{:S(2)}, u32[]{:S(2)}) async-start(bf16[192,16,256]{2,0,1:T(8,128)(2,1)} %bitcast.108), calls=%async_computation.2 | async-start | bytes 3145728 | tf_op jit(solution)/shard_map/all_to_all | solution.py:106
  213.3 11.8 %all-to-all-start.4 = ((f32[16,1,16]{2,1,0:T(1,128)}), f32[16,1,16]{2,1,0:T(1,128)S(1)}, u32[]{:S(2)}, u32[]{:S(2)}) async-start(f32[16,1,16]{2,1,0:T(1,128)} %broadcast_in_dim.9), calls=%async_computation.5 | async-start | bytes 16384 | tf_op jit(solution)/shard_map/all_to_all | solution.py:17
Sparse Core Ops, SparseCore 0:
  12.0 96.0 all-gather.1
  127.0 136.1 reduce-scatter.1
where the time goes:
time: 300 us; the launch traced here: 299 us
  waiting for transfers between devices  140 us (47%)
  blocking collectives  74.3 us (25%)
  matrix products  25.6 us (9%)
  starting transfers between devices  22.6 us (8%)
  other arithmetic  15.4 us (5%)
  between operations  14.4 us (5%)
  local copies, waits for them, and re-layouts  6.32 us (2%)
    all_to_all x1, waiting for transfers between devices, body(): lax.all_to_all(first_grad, 'group', split_axis=1, concat_axis=0, tiled=True)  38 us
    all_to_all x1, waiting for transfers between devices, body(): lax.all_to_all(projected, 'group', split_axis=0, concat_axis=1, tiled=True)  37.7 us
    all_gather x1, waiting for transfers between devices, body(): lax.all_gather(jnp.concatenate([down_weight, up_weight], axis=0), 'row',...  37 us
    reduce_scatter x1, waiting for transfers between devices, body(): weight_rows = lax.psum_scatter(slab, 'row', scatter_dimension=1, tiled=True)  19.4 us
    all_to_all x1, blocking collectives, body(): lax.all_to_all(jnp.concatenate([proj_pieces, bias_pieces], axis=1), 'row'...  18.1 us
    all_to_all x1, blocking collectives, body(): lax.all_to_all(jnp.broadcast_to(last[None], (row_count_axis,) + last.shap...  15.9 us
    all_to_all x1, blocking collectives, group_all_reduce(): lax.all_to_all(pieces, 'group', 0, 0, tiled=True).astype(jnp.float32)  15.7 us
    all_to_all x1, blocking collectives, exchange_sum(): mine = jnp.sum(lax.all_to_all(pieces, axis, 0, 0, tiled=True), axis=0)  13 us
  transfers between devices with their start and end apart: 5, of which 5 were waited for; matrix products, arithmetic and copies ran while one was open for 8% of the time, Pallas kernels for 0%

commit v1 on v0

--- a/solution.py
+++ b/solution.py
@@ -54,8 +54,14 @@
     first_wide = first.astype(jnp.float32)
     crossed = first
     stored = []
-    weights_full = lax.all_gather(
-        jnp.concatenate([down_weight, up_weight], axis=0), "row", axis=1, tiled=True
+    weights_full = jnp.concatenate(
+        lax.all_to_all(
+            jnp.stack([jnp.concatenate([down_weight, up_weight], axis=0)] * lax.axis_size("row")),
+            "row",
+            0,
+            0,
+        ),
+        axis=1,
     )
     for layer_index in range(layers):
         down_full, up_full = (weights_full[layer_index], weights_full[layers + layer_index])

time: 300 us -> 367 us (1.22)
  waiting for transfers between devices: 140 us -> 195 us
  starting transfers between devices: 22.6 us -> 29.6 us
  local copies, waits for them, and re-layouts: 6.32 us -> 13.3 us
    all_to_all x0 -> x1, waiting for transfers between devices: none -> 92.1 us  [body(): lax.all_to_all(jnp.stack([jnp.concatenate([down_weight, up_weight], axis=...]
    all_gather x1 -> x0, waiting for transfers between devices: 37 us -> none  [body(): lax.all_gather(jnp.concatenate([down_weight, up_weight], axis=0), 'row',...]
    all_to_all x0 -> x1, starting transfers between devices: none -> 9.95 us  [body(): lax.all_to_all(jnp.stack([jnp.concatenate([down_weight, up_weight], axis=...]
  transfers between devices with their start and end apart: 5 -> 5, of which waited for: 5 -> 5; matrix products, arithmetic and copies ran while one was open for 8% -> 3% of each run, Pallas kernels for 0% -> 0%
where the time goes in v1:
time: 367 us; the launch traced here: 366 us
  waiting for transfers between devices  195 us (53%)
  blocking collectives  77.8 us (21%)
  starting transfers between devices  29.6 us (8%)
  matrix products  22.7 us (6%)
  between operations  14.4 us (4%)
  other arithmetic  13.9 us (4%)
  local copies, waits for them, and re-layouts  13.3 us (4%)
    all_to_all x1, waiting for transfers between devices, body(): lax.all_to_all(jnp.stack([jnp.concatenate([down_weight, up_weight], axis=...  92.1 us
    all_to_all x1, waiting for transfers between devices, body(): lax.all_to_all(projected, 'group', split_axis=0, concat_axis=1, tiled=True)  38 us
    all_to_all x1, waiting for transfers between devices, body(): lax.all_to_all(first_grad, 'group', split_axis=1, concat_axis=0, tiled=True)  37.2 us
    all_to_all x1, blocking collectives, body(): lax.all_to_all(jnp.concatenate([proj_pieces, bias_pieces], axis=1), 'row'...  21.3 us
    reduce_scatter x1, waiting for transfers between devices, body(): weight_rows = lax.psum_scatter(slab, 'row', scatter_dimension=1, tiled=True)  18.9 us
    all_to_all x1, blocking collectives, body(): lax.all_to_all(jnp.broadcast_to(last[None], (row_count_axis,) + last.shap...  16.1 us
    all_to_all x1, blocking collectives, group_all_reduce(): lax.all_to_all(pieces, 'group', 0, 0, tiled=True).astype(jnp.float32)  15.9 us
    all_to_all x1, blocking collectives, exchange_sum(): mine = jnp.sum(lax.all_to_all(pieces, axis, 0, 0, tiled=True), axis=0)  12.9 us
  transfers between devices with their start and end apart: 5, of which 5 were waited for; matrix products, arithmetic and copies ran while one was open for 3% of the time, Pallas kernels for 0%

profile of v1, /device:TPU:16, one launch (start us, length us, event | category | flops | bytes accessed | tf_op | source)
XLA Modules:
  0.0 366.3 jit_solution(816247132235613609)
XLA Ops:
  7.2 0.0 copy-start
  7.2 1.4 fusion.17
  8.6 0.7 compare_select_fusion
  9.3 8.9 %scatter_custom_fusion = bf16[3072,128]{1,0:T(8,128)(2,1)S(1)} fusion(s32[3072]{0:T(1024)S(1)} %bitcast.120, f32[3072,128]{1,0:T(8,128)} %param.11, f32[128]{0:T(128)S(1)} %get-tuple-element.28, f32[128]{0:T(128)S(1)} %get-tuple-element.27, bf16[]{:T(256)} %constant.1.clone.1), kind=kCustom, calls=%fused_computation.48 | custom fusion | flops 1179648 | bytes 2360322 | tf_op jit(solution)/shard_map/scatter | solution.py:49
  18.2 0.0 copy-done
  18.2 0.0 copy-start.5
  18.3 1.7 convolution_convert_fusion.4
  20.0 0.0 copy-done.5
  20.0 11.5 %all-to-all-start = ((bf16[16,192,256]{2,1,0:T(8,128)(2,1)}), bf16[16,192,256]{2,1,0:T(8,128)(2,1)S(1)}, u32[]{:S(2)}, u32[]{:S(2)}) async-start(bf16[16,192,256]{2,1,0:T(8,128)(2,1)} %bitcast.6), calls=%async_computation | async-start | bytes 3145728 | tf_op jit(solution)/shard_map/all_to_all | solution.py:53
  31.5 0.0 copy-done.7
  31.5 0.0 copy-done.8
  31.5 38.0 %all-to-all-done = bf16[16,192,256]{2,1,0:T(8,128)(2,1)S(1)} async-done(((bf16[16,192,256]{2,1,0:T(8,128)(2,1)}), bf16[16,192,256]{2,1,0:T(8,128)(2,1)S(1)}, u32[]{:S(2)}, u32[]{:S(2)}) %all-to-all-start) | async-done | bytes 1572896 | tf_op jit(solution)/shard_map/all_to_all | solution.py:53
  69.5 3.0 stack.32
  72.5 10.0 %all-to-all-start.1 = ((bf16[32,4,128,128]{3,2,1,0:T(8,128)(2,1)}), bf16[32,4,128,128]{3,2,1,0:T(8,128)(2,1)}, u32[]{:S(2)}, u32[]{:S(2)}) async-start(bf16[32,4,128,128]{3,2,1,0:T(8,128)(2,1)} %stack.32), calls=%async_computation.1 | async-start | bytes 8388608 | tf_op jit(solution)/shard_map/all_to_all | solution.py:58
  82.5 0.2 reduce-scatter.2.cloned.1.call-start
  82.7 0.0 copy-done.6
  82.7 0.0 copy-done.9
  82.8 0.2 copy.47
  83.0 92.1 %all-to-all-done.1 = bf16[32,4,128,128]{3,2,1,0:T(8,128)(2,1)} async-done(((bf16[32,4,128,128]{3,2,1,0:T(8,128)(2,1)}), bf16[32,4,128,128]{3,2,1,0:T(8,128)(2,1)}, u32[]{:S(2)}, u32[]{:S(2)}) %all-to-all-start.1) | async-done | bytes 4194336 | tf_op jit(solution)/shard_map/all_to_all | solution.py:58
  175.0 2.8 fusion.28
  177.8 0.0 copy-start.3
  177.8 0.6 convolution_convert_fusion.8
  178.4 2.4 fusion.11
  180.7 0.6 convolution_convert_fusion.7
  181.3 0.0 copy-start.11
  181.3 2.7 multiply_reduce_fusion
  184.0 0.6 fusion.16
  184.6 0.2 copy.48
  184.8 0.6 convolution_convert_fusion.6
  185.4 0.8 fusion.9
  186.2 2.6 fusion.15
  188.8 0.6 convolution_convert_fusion.5
  189.3 0.8 fusion.6
  190.1 0.8 fusion.8
  190.9 0.8 fusion.7
  191.7 2.2 pad_maximum_fusion
  193.9 0.0 reduce-scatter.2.cloned.1.call-update
  193.9 1.2 copy-done.4
  195.1 4.6 %fusion.5 = bf16[192,4096]{1,0:T(8,128)(2,1)S(1)} fusion(f32[192,4096]{1,0:T(8,128)} %get-tuple-element.33, bf16[192,128]{1,0:T(8,128)(2,1)S(1)} %convolution_convert_fusion.5, bf16[4096,128]{1,0:T(8,128)(2,1)S(1)} %bitcast.100, f32[192,4096]{1,0:T(8,128)} %get-tuple-element.32, f32[192,4096]{1,0:T(8,128)} %get-tuple-element.30, f32[192]{0:T(256)S(1)} %fusion.26, ...), kind=kOutput, calls=%fused_computation.15 | convolution fusion | flops 209977344 | bytes 12124928 | tf_op jit(solution)/shard_map/dot_general | solution.py:101
  199.7 1.3 copy.55
  201.1 4.5 %all-to-all-start.2 = ((bf16[192,16,256]{2,0,1:T(8,128)(2,1)}), bf16[192,16,256]{2,0,1:T(8,128)(2,1)}, u32[]{:S(2)}, u32[]{:S(2)}) async-start(bf16[192,16,256]{2,0,1:T(8,128)(2,1)} %bitcast.107), calls=%async_computation.3 | async-start | bytes 3145728 | tf_op jit(solution)/shard_map/all_to_all | solution.py:112
  205.6 0.5 convert_reduce_fusion
  206.2 37.2 %all-to-all-done.2 = bf16[192,16,256]{2,0,1:T(8,128)(2,1)} async-done(((bf16[192,16,256]{2,0,1:T(8,128)(2,1)}), bf16[192,16,256]{2,0,1:T(8,128)(2,1)}, u32[]{:S(2)}, u32[]{:S(2)}) %all-to-all-start.2) | async-done | bytes 1572896 | tf_op jit(solution)/shard_map/all_to_all | solution.py:112
  243.4 2.1 fusion.30
  245.6 0.1 all_to_all.68
  245.7 21.3 %all_to_all.86 = f32[32,1,1280]{2,1,0:T(1,128)S(1)} all-to-all(f32[32,1,1280]{2,1,0:T(1,128)S(1)} %all_to_all.68), channel_id=1, replica_groups=mesh['group'=16,'row'=32] {'row'}, dimensions={0} | all-to-all | bytes 327680 | tf_op jit(solution)/shard_map/all_to_all | solution.py:123
  267.0 0.1 reduce_sum.60
  267.1 0.1 all_to_all.70
  267.2 12.9 %all_to_all.87 = f32[16,1,16]{2,1,0:T(1,128)S(1)} all-to-all(f32[16,1,16]{2,1,0:T(1,128)S(1)} %all_to_all.70), channel_id=1, replica_groups=mesh['group'=16,'row'=32] {'group'}, dimensions={0} | all-to-all | bytes 2048 | tf_op jit(solution)/shard_map/all_to_all | solution.py:15
  280.1 0.6 broadcast_in_dim.9
  280.7 3.5 all-to-all-start.5
  284.2 8.3 %all-to-all-done.5 = f32[16,1,16]{2,1,0:T(1,128)S(1)} async-done(((f32[16,1,16]{2,1,0:T(1,128)}), f32[16,1,16]{2,1,0:T(1,128)S(1)}, u32[]{:S(2)}, u32[]{:S(2)}) %all-to-all-start.5) | async-done | bytes 1056 | tf_op jit(solution)/shard_map/all_to_all | solution.py:17
  292.5 0.5 broadcast.41
  293.1 0.7 reduce.6
  293.7 0.1 reshape.132
  293.8 0.1 broadcast_in_dim.10
  293.9 16.1 %all_to_all.88 = f32[32,1,1280]{2,1,0:T(1,128)S(1)} all-to-all(f32[32,1,1280]{2,1,0:T(1,128)S(1)} %broadcast_in_dim.10), channel_id=1, replica_groups=mesh['group'=16,'row'=32] {'row'}, dimensions={0} | all-to-all | bytes 327680 | tf_op jit(solution)/shard_map/all_to_all | solution.py:130
  310.0 0.7 reshape.133
  310.7 0.6 reshape.134
  311.4 18.9 %reduce-scatter.2.cloned.1.call-done = bf16[4,128,128]{2,1,0:T(8,128)(2,1)} async-done(((bf16[4,4096,128]{2,1,0:T(8,128)(2,1)}), bf16[4,128,128]{2,1,0:T(8,128)(2,1)}) %reduce-scatter.2.cloned.1.call-update) | async-done | bytes 131088 | tf_op jit(solution)/shard_map/reduce_scatter | solution.py:110
  330.2 0.9 copy_bitcast_fusion.2
  331.2 15.9 %all_to_all.89 = bf16[16,4,8,128]{3,2,1,0:T(8,128)(2,1)S(1)} all-to-all(bf16[16,4,8,128]{3,2,1,0:T(8,128)(2,1)S(1)} %copy_bitcast_fusion.2), channel_id=1, replica_groups=mesh['group'=16,'row'=32] {'group'}, dimensions={0} | all-to-all | bytes 262144 | tf_op jit(solution)/shard_map/all_to_all | solution.py:23
  347.1 11.6 %all_to_all.90 = bf16[16,4,8,128]{3,2,1,0:T(8,128)(2,1)S(1)} all-to-all(bf16[16,4,8,128]{3,2,1,0:T(8,128)(2,1)S(1)} %broadcast_in_dim.11), channel_id=1, replica_groups=mesh['group'=16,'row'=32] {'group'}, dimensions={0} | all-to-all | bytes 262144 | tf_op jit(solution)/shard_map/all_to_all | solution.py:25
  358.8 0.7 slice_bitcast_fusion
  (32 shorter events, 0.3 us)
Async XLA Ops:
  7.2 11.1 %copy-start = (bf16[128,256]{1,0:T(8,128)(2,1)S(1)}, bf16[128,256]{1,0:T(8,128)(2,1)}, u32[]{:S(2)}) copy-start(bf16[128,256]{1,0:T(8,128)(2,1)} %param.15) | copy-start | bytes 196612
  18.2 1.7 copy-start.5
  20.0 11.5 %copy-start.7 = (bf16[2,128,128]{2,1,0:T(8,128)(2,1)S(1)}, bf16[2,128,128]{2,1,0:T(8,128)(2,1)}, u32[]{:S(2)}) copy-start(bf16[2,128,128]{2,1,0:T(8,128)(2,1)} %param.18) | copy-start | bytes 196612
  20.0 11.5 %copy-start.8 = (bf16[2,128,128]{2,1,0:T(8,128)(2,1)S(1)}, bf16[2,128,128]{2,1,0:T(8,128)(2,1)}, u32[]{:S(2)}) copy-start(bf16[2,128,128]{2,1,0:T(8,128)(2,1)} %param.17) | copy-start | bytes 196612
  20.0 49.5 %all-to-all-start = ((bf16[16,192,256]{2,1,0:T(8,128)(2,1)}), bf16[16,192,256]{2,1,0:T(8,128)(2,1)S(1)}, u32[]{:S(2)}, u32[]{:S(2)}) async-start(bf16[16,192,256]{2,1,0:T(8,128)(2,1)} %bitcast.6), calls=%async_computation | async-start | bytes 3145728 | tf_op jit(solution)/shard_map/all_to_all | solution.py:53
  72.5 10.2 %copy-start.6 = (f32[4096]{0:T(1024)S(1)}, f32[4096]{0:T(1024)}, u32[]{:S(2)}) copy-start(f32[4096]{0:T(1024)} %param.20) | copy-start | bytes 49156
  72.5 10.2 %copy-start.9 = (f32[2,4096]{1,0:T(2,128)S(1)}, f32[2,4096]{1,0:T(2,128)}, u32[]{:S(2)}) copy-start(f32[2,4096]{1,0:T(2,128)} %param.19) | copy-start | bytes 98308
  72.5 102.5 %all-to-all-start.1 = ((bf16[32,4,128,128]{3,2,1,0:T(8,128)(2,1)}), bf16[32,4,128,128]{3,2,1,0:T(8,128)(2,1)}, u32[]{:S(2)}, u32[]{:S(2)}) async-start(bf16[32,4,128,128]{3,2,1,0:T(8,128)(2,1)} %stack.32), calls=%async_computation.1 | async-start | bytes 8388608 | tf_op jit(solution)/shard_map/all_to_all | solution.py:58
  82.5 247.8 %reduce-scatter.2.cloned.1.call-start = ((), (), s32[]{:S(2)}) async-start(), calls=%async_computation.10 | async-start | bytes 4325376 | tf_op jit(solution)/shard_map/reduce_scatter | solution.py:110
  177.8 2.9 copy-start.3
  181.3 2.7 copy-start.11
  184.0 0.8 copy-start.10
  188.8 2.1 copy-start.1
  193.9 1.2 copy-start.4
  201.1 4.5 %copy-start.2 = (bf16[192,4096]{1,0:T(8,128)(2,1)S(1)}, bf16[192,4096]{1,0:T(8,128)(2,1)}, u32[]{:S(2)}) copy-start(bf16[192,4096]{1,0:T(8,128)(2,1)} %copy-done.1) | copy-start | bytes 4718596
  201.1 42.3 %all-to-all-start.2 = ((bf16[192,16,256]{2,0,1:T(8,128)(2,1)}), bf16[192,16,256]{2,0,1:T(8,128)(2,1)}, u32[]{:S(2)}, u32[]{:S(2)}) async-start(bf16[192,16,256]{2,0,1:T(8,128)(2,1)} %bitcast.107), calls=%async_computation.3 | async-start | bytes 3145728 | tf_op jit(solution)/shard_map/all_to_all | solution.py:112
  280.7 11.8 %all-to-all-start.5 = ((f32[16,1,16]{2,1,0:T(1,128)}), f32[16,1,16]{2,1,0:T(1,128)S(1)}, u32[]{:S(2)}, u32[]{:S(2)}) async-start(f32[16,1,16]{2,1,0:T(1,128)} %broadcast_in_dim.9), calls=%async_computation.6 | async-start | bytes 16384 | tf_op jit(solution)/shard_map/all_to_all | solution.py:17
Sparse Core Ops, SparseCore 0:
  194.1 136.1 reduce-scatter.1
